TPU v7x, 32 devices: a whole 2x2x4 slice. The times are simulated.
32 devices in a mesh: row: 2 (over x), col: 4 (over z), tok: 4 (over y, core).
Axes of the slice: x: 2, y: 2, z: 4, core: 2. Of those that a mesh axis runs over, the one named last changes fastest.
Arguments:
- activations: bfloat16 [4096, 2048], P(('row', 'col', 'tok')), may hold values from -6 to 6
- norm_gain: float32 [2048], replicated, may hold values from 0.1 to 1.9
- routes: int32 [4096, 8], P(('row', 'col', 'tok')), may hold values from 0 to 127, all different within a row; in each aligned block of 128 rows (0 to 127, 128 to 255, ...) at most 10 rows name the same one
- route_weights: float32 [4096, 8], P(('row', 'col', 'tok')), may hold values from 0.05 to 1
- gate_up_weight: bfloat16 [128, 2, 768, 2048], P(('row', 'col'), None, 'tok'), may hold values from -0.125 to 0.125
- down_weight: bfloat16 [128, 768, 2048], P(('row', 'col'), 'tok'), may hold values from -0.21875 to 0.21875
Outputs:
- expert_mix: bfloat16 [4096, 2048], P(('row', 'col', 'tok'))
Inputs may be any that keep to these rules, and one draw needn't show every extreme that they name: `routes`: within the rows of one device no expert is named by more than 10 rows, a bound that some block reaches.
All inputs are finite; a program needn't handle non-finite values.
Results may differ from a plain program's by a relative error of at most 0.0085.
Values may be sent and summed in bfloat16 or wider, within the bound.
No kernel may reach another device: no remote copies, remote signals or barrier semaphores. Data moves between devices by JAX's collectives and lax.ppermute only.
A program may use at most 384 MiB of HBM per device.

v0:
```python
import math
import jax
import jax.numpy as jnp
from jax import lax
from jax.sharding import PartitionSpec as P

CAP = 10
PIECES = 4
EPSILON = 1e-06
ALL = ("row", "col", "tok")


def rank_in_block(block_routes, experts):
    onehot = (block_routes[:, None] == jnp.arange(experts, dtype=jnp.int32)[None, :]).astype(
        jnp.int32
    )
    before = jnp.cumsum(onehot, axis=0) - onehot
    return jnp.sum(before * onehot, axis=1)


def rms_normed(activations, norm_gain):
    values = activations.astype(jnp.float32)
    scale = lax.rsqrt(jnp.mean(values * values, axis=-1, keepdims=True) + EPSILON)
    return (values * scale * norm_gain).astype(jnp.bfloat16)


def local(activations, norm_gain, routes, route_weights, gate_up_weight, down_weight):
    count, features = activations.shape
    chosen = routes.shape[1]
    holding = gate_up_weight.shape[0]
    row_count = lax.axis_size("row")
    col_count = lax.axis_size("col")
    tok_count = lax.axis_size("tok")
    owners = row_count * col_count
    experts = holding * owners
    devices = owners * tok_count
    owner = lax.axis_index("row") * col_count + lax.axis_index("col")
    assert count < 256
    normed = rms_normed(activations, norm_gain)
    gates = route_weights / jnp.sum(route_weights, axis=1, keepdims=True)
    flat_routes = routes.reshape(-1)
    target = flat_routes * CAP + rank_in_block(flat_routes, experts)
    token_ids = jnp.arange(count * chosen, dtype=jnp.int32) // chosen
    source = jnp.full((experts * CAP,), count, jnp.int32).at[target].set(token_ids)
    extra = -(-(experts * CAP) // features)
    extra = -(-extra // 8) * 8
    stride = count + extra
    table_rows = jnp.zeros((extra * features,), jnp.bfloat16)
    table_rows = table_rows.at[: experts * CAP].set(source.astype(jnp.bfloat16))
    packed = jnp.concatenate([normed, table_rows.reshape(extra, features)], axis=0)
    every = lax.all_gather(packed, ALL, axis=0, tiled=True)
    tables = every.reshape(devices, stride, features)[:, count:, :].reshape(devices, -1)
    tables = lax.dynamic_slice_in_dim(
        tables[:, : experts * CAP], owner * holding * CAP, holding * CAP, axis=1
    ).astype(jnp.int32)
    rows = tables + (jnp.arange(devices, dtype=jnp.int32) * stride)[:, None]
    rows = rows.reshape(owners, tok_count, holding, CAP).transpose(2, 1, 0, 3).reshape(-1)
    rows = rows.reshape(holding, -1)
    pieces = math.gcd(holding, PIECES)
    width = holding // pieces
    returned = []
    sums = []
    for piece in range(pieces):
        span = slice(piece * width, (piece + 1) * width)
        picked = jnp.take(every, rows[span].reshape(-1), axis=0, mode="clip")
        picked = picked.reshape(width, tok_count * owners * CAP, features)
        both = jnp.einsum(
            "jrd,jgfd->jrgf", picked, gate_up_weight[span], preferred_element_type=jnp.float32
        )
        hidden = (jax.nn.silu(both[:, :, 0, :]) * both[:, :, 1, :]).astype(jnp.bfloat16)
        partial = jnp.einsum(
            "jrf,jfd->jrd", hidden, down_weight[span], preferred_element_type=jnp.float32
        )
        partial = partial.astype(jnp.bfloat16)
        if sums:
            partial, _ = lax.optimization_barrier((partial, (sums[-1], returned[:-1])))
        sums.append(lax.psum_scatter(partial, "tok", scatter_dimension=1, tiled=True))
        summed = sums[-1].reshape(width, owners, CAP, features).transpose(1, 0, 2, 3)
        summed = summed.reshape(owners, width * CAP, features)
        returned.append(
            lax.all_to_all(summed, ("row", "col"), split_axis=0, concat_axis=0, tiled=True)
        )
    returned = jnp.concatenate(returned, axis=1)
    picked_back = jnp.take(returned.reshape(experts * CAP, features), target, axis=0)
    picked_back = picked_back.reshape(count, chosen, features)
    mixed = jnp.einsum("tk,tkd->td", gates, picked_back.astype(jnp.float32))
    return mixed.astype(jnp.bfloat16)


def solution(mesh):
    in_specs = (
        P(("row", "col", "tok"), None),
        P(),
        P(("row", "col", "tok"), None),
        P(("row", "col", "tok"), None),
        P(("row", "col"), None, "tok", None),
        P(("row", "col"), "tok", None),
    )
    out_specs = P(("row", "col", "tok"), None)
    return jax.shard_map(local, mesh=mesh, in_specs=in_specs, out_specs=out_specs, check_vma=False)
```

profile of v0, /device:TPU:0, one launch (start us, length us, event | category | flops | bytes accessed | tf_op | source)
XLA Modules:
  0.0 457.8 jit_solution(16420601011597710427)
XLA Ops:
  10.6 4.3 scatter_custom_fusion
  16.2 122.6 %all-gather.2.cloned.1.call-done = bf16[4352,2048]{1,0:T(8,128)(2,1)} async-done(((bf16[136,2048]{1,0:T(8,128)(2,1)}), bf16[4352,2048]{1,0:T(8,128)(2,1)}) %all-gather.2.cloned.1.call-update) | async-done | bytes 17825808 | tf_op jit(solution)/shard_map/all_gather | solution.py:51
  141.2 19.2 %gather_fusion = bf16[1280,2048]{1,0:T(8,128)(2,1)} fusion(bf16[4352,2048]{1,0:T(8,128)(2,1)} %all-gather.2.cloned.1.call-done, s32[2048]{0:T(1024)S(1)} %pad_clamp_fusion.3), kind=kCustom, calls=%fused_computation | custom fusion | bytes 10490880 | tf_op jit(solution)/shard_map/jit(_take)/gather | solution.py:65
  160.4 7.8 %fusion.6 = f32[4,320,2,192]{1,3,2,0:T(8,128)S(1)} fusion(bf16[4,320,2048,1]{2,1,3,0:T(8,128)(2,1)} %bitcast.124, bf16[16,2,192,2048]{3,2,1,0:T(8,128)(2,1)} %param.12), kind=kOutput, calls=%fused_computation.12 | convolution fusion | flops 2013265920 | bytes 13500416 | tf_op jit(solution)/shard_map/jrd,jgfd->jrgf/dot_general | solution.py:67
  168.2 5.8 %convolution_convert_fusion.3 = bf16[4,320,2048]{2,1,0:T(8,128)(2,1)} fusion(bf16[16,192,2048]{2,1,0:T(8,128)(2,1)} %param.13, f32[4,320,2,192]{1,3,2,0:T(8,128)S(1)} %fusion.6), kind=kOutput, calls=%fused_computation.21 | convolution fusion | flops 1010728960 | bytes 10354688 | tf_op jit(solution)/shard_map/jrf,jfd->jrd/dot_general | solution.py:71
  174.2 16.3 %fusion.49 = (bf16[4,2,192,2048]{3,2,1,0:T(8,128)(2,1)}, bf16[4,2,192,2048]{3,2,1,0:T(8,128)(2,1)}, bf16[4,2,192,2048]{3,2,1,0:T(8,128)(2,1)}) fusion(bf16[16,2,192,2048]{3,2,1,0:T(8,128)(2,1)} %param.12), kind=kLoop, calls=%fused_computation.91 | loop fusion | bytes 37748736 | tf_op jit(solution)/shard_map/slice | solution.py:68
  190.6 20.0 %gather_fusion.1 = bf16[1280,2048]{1,0:T(8,128)(2,1)} fusion(bf16[4352,2048]{1,0:T(8,128)(2,1)} %all-gather.2.cloned.1.call-done, s32[2048]{0:T(1024)S(1)} %pad_clamp_fusion.2), kind=kCustom, calls=%fused_computation.1 | custom fusion | bytes 10490880 | tf_op jit(solution)/shard_map/jit(_take)/gather | solution.py:65
  210.7 7.8 %fusion.4 = f32[4,320,2,192]{1,3,0,2:T(8,128)S(1)} fusion(bf16[4,320,2048,1]{2,1,0,3:T(8,128)(2,1)} %bitcast.122, bf16[4,2,192,2048]{3,2,1,0:T(8,128)(2,1)} %get-tuple-element.23), kind=kOutput, calls=%fused_computation.10 | convolution fusion | flops 2013265920 | bytes 13500416 | tf_op jit(solution)/shard_map/jrd,jgfd->jrgf/dot_general | solution.py:67
  218.5 5.8 %convolution_convert_fusion.2 = bf16[4,320,2048]{2,1,0:T(8,128)(2,1)} fusion(bf16[16,192,2048]{2,1,0:T(8,128)(2,1)} %param.13, f32[4,320,2,192]{1,3,0,2:T(8,128)S(1)} %fusion.4), kind=kOutput, calls=%fused_computation.20 | convolution fusion | flops 1010728960 | bytes 10354688 | tf_op jit(solution)/shard_map/jrf,jfd->jrd/dot_general | solution.py:71
  227.3 1.8 copy.79
  229.1 5.0 %all-to-all-start = ((bf16[8,40,2048]{2,1,0:T(8,128)(2,1)}), bf16[8,40,2048]{2,1,0:T(8,128)(2,1)S(1)}, u32[]{:S(2)}, u32[]{:S(2)}) async-start(bf16[8,40,2048]{2,1,0:T(8,128)(2,1)} %copy.79), calls=%async_computation.1 | async-start | bytes 2621440 | tf_op jit(solution)/shard_map/all_to_all | solution.py:81
  234.5 20.5 %gather_fusion.2 = bf16[1280,2048]{1,0:T(8,128)(2,1)} fusion(bf16[4352,2048]{1,0:T(8,128)(2,1)} %all-gather.2.cloned.1.call-done, s32[2048]{0:T(1024)S(1)} %pad_clamp_fusion.1), kind=kCustom, calls=%fused_computation.2 | custom fusion | bytes 10490880 | tf_op jit(solution)/shard_map/jit(_take)/gather | solution.py:65
  255.0 7.9 %fusion.2 = f32[4,320,2,192]{1,3,0,2:T(8,128)S(1)} fusion(bf16[4,320,2048,1]{2,1,0,3:T(8,128)(2,1)} %bitcast.123, bf16[4,2,192,2048]{3,2,1,0:T(8,128)(2,1)} %get-tuple-element.25), kind=kOutput, calls=%fused_computation.8 | convolution fusion | flops 2013265920 | bytes 13500416 | tf_op jit(solution)/shard_map/jrd,jgfd->jrgf/dot_general | solution.py:67
  262.9 5.9 %convolution_convert_fusion.1 = bf16[4,320,2048]{2,1,0:T(8,128)(2,1)} fusion(bf16[16,192,2048]{2,1,0:T(8,128)(2,1)} %param.13, f32[4,320,2,192]{1,3,0,2:T(8,128)S(1)} %fusion.2), kind=kOutput, calls=%fused_computation.19 | convolution fusion | flops 1010728960 | bytes 10354688 | tf_op jit(solution)/shard_map/jrf,jfd->jrd/dot_general | solution.py:71
  268.8 9.1 %reduce-scatter.7.cloned.1.call-done = bf16[4,80,2048]{2,1,0:T(8,128)(2,1)} async-done(((bf16[4,320,2048]{2,1,0:T(8,128)(2,1)}), bf16[4,80,2048]{2,1,0:T(8,128)(2,1)}) %reduce-scatter.7.cloned.1.call-update) | async-done | bytes 1310736 | tf_op jit(solution)/shard_map/reduce_scatter | solution.py:77
  280.9 1.8 copy.85
  282.7 5.5 %all-to-all-start.1 = ((bf16[8,40,2048]{2,1,0:T(8,128)(2,1)}), bf16[8,40,2048]{2,1,0:T(8,128)(2,1)S(1)}, u32[]{:S(2)}, u32[]{:S(2)}) async-start(bf16[8,40,2048]{2,1,0:T(8,128)(2,1)} %copy.85), calls=%async_computation.3 | async-start | bytes 2621440 | tf_op jit(solution)/shard_map/all_to_all | solution.py:81
  288.8 20.2 %gather_fusion.3 = bf16[1280,2048]{1,0:T(8,128)(2,1)} fusion(bf16[4352,2048]{1,0:T(8,128)(2,1)} %all-gather.2.cloned.1.call-done, s32[2048]{0:T(1024)S(1)} %pad_clamp_fusion), kind=kCustom, calls=%fused_computation.3 | custom fusion | bytes 10490880 | tf_op jit(solution)/shard_map/jit(_take)/gather | solution.py:65
  309.0 7.9 %fusion = f32[4,320,2,192]{1,3,0,2:T(8,128)S(1)} fusion(bf16[4,320,2048,1]{2,1,0,3:T(8,128)(2,1)} %bitcast.121, bf16[4,2,192,2048]{3,2,1,0:T(8,128)(2,1)} %get-tuple-element.24), kind=kOutput, calls=%fused_computation.6 | convolution fusion | flops 2013265920 | bytes 13500416 | tf_op jit(solution)/shard_map/jrd,jgfd->jrgf/dot_general | solution.py:67
  316.9 5.9 %convolution_convert_fusion = bf16[4,320,2048]{2,1,0:T(8,128)(2,1)} fusion(bf16[16,192,2048]{2,1,0:T(8,128)(2,1)} %param.13, f32[4,320,2,192]{1,3,0,2:T(8,128)S(1)} %fusion), kind=kOutput, calls=%fused_computation.18 | convolution fusion | flops 1010728960 | bytes 10354688 | tf_op jit(solution)/shard_map/jrf,jfd->jrd/dot_general | solution.py:71
  322.8 8.8 %reduce-scatter.9.cloned.1.call-done = bf16[4,80,2048]{2,1,0:T(8,128)(2,1)} async-done(((bf16[4,320,2048]{2,1,0:T(8,128)(2,1)}), bf16[4,80,2048]{2,1,0:T(8,128)(2,1)}) %reduce-scatter.9.cloned.1.call-update) | async-done | bytes 1310736 | tf_op jit(solution)/shard_map/reduce_scatter | solution.py:77
  331.7 2.3 copy.89
  334.7 1.9 copy.91
  336.6 5.8 %all-to-all-start.2 = ((bf16[8,40,2048]{2,1,0:T(8,128)(2,1)}), bf16[8,40,2048]{2,1,0:T(8,128)(2,1)}, u32[]{:S(2)}, u32[]{:S(2)}) async-start(bf16[8,40,2048]{2,1,0:T(8,128)(2,1)} %copy.91), calls=%async_computation.5 | async-start | bytes 2621440 | tf_op jit(solution)/shard_map/all_to_all | solution.py:81
  342.4 43.3 %reduce-scatter.11.cloned.1.call-done = bf16[4,80,2048]{2,1,0:T(8,128)(2,1)} async-done(((bf16[4,320,2048]{2,1,0:T(8,128)(2,1)}), bf16[4,80,2048]{2,1,0:T(8,128)(2,1)}) %reduce-scatter.11.cloned.1.call-update) | async-done | bytes 1310736 | tf_op jit(solution)/shard_map/reduce_scatter | solution.py:77
  385.6 2.3 copy.95
  388.7 1.8 copy.97
  390.5 5.5 %all-to-all-start.3 = ((bf16[8,40,2048]{2,1,0:T(8,128)(2,1)}), bf16[8,40,2048]{2,1,0:T(8,128)(2,1)}, u32[]{:S(2)}, u32[]{:S(2)}) async-start(bf16[8,40,2048]{2,1,0:T(8,128)(2,1)} %copy.97), calls=%async_computation.7 | async-start | bytes 2621440 | tf_op jit(solution)/shard_map/all_to_all | solution.py:81
  396.5 31.9 %all-to-all-done.3 = bf16[8,40,2048]{2,1,0:T(8,128)(2,1)} async-done(((bf16[8,40,2048]{2,1,0:T(8,128)(2,1)}), bf16[8,40,2048]{2,1,0:T(8,128)(2,1)}, u32[]{:S(2)}, u32[]{:S(2)}) %all-to-all-start.3) | async-done | bytes 1310752 | tf_op jit(solution)/shard_map/all_to_all | solution.py:81
  428.4 6.0 %pad_maximum_fusion = bf16[8,160,2048]{2,1,0:T(8,128)(2,1)} fusion(bf16[8,40,2048]{2,1,0:T(8,128)(2,1)} %all-to-all-done.3, bf16[8,40,2048]{2,1,0:T(8,128)(2,1)} %all-to-all-done.2, bf16[8,40,2048]{2,1,0:T(8,128)(2,1)S(1)} %all-to-all-done.1, bf16[8,40,2048]{2,1,0:T(8,128)(2,1)S(1)} %all-to-all-done), kind=kLoop, calls=%fused_computation.14 | loop fusion | flops 20971520 | bytes 10485760 | tf_op jit(solution)/shard_map/concatenate | solution.py:83
  434.4 12.0 %gather_fusion.4 = bf16[1024,2048]{1,0:T(8,128)(2,1)} fusion(bf16[1280,2048]{1,0:T(8,128)(2,1)} %bitcast.120, s32[1024]{0:T(1024)S(1)} %broadcast_clamp_fusion), kind=kCustom, calls=%fused_computation.4 | custom fusion | bytes 8392704 | tf_op jit(solution)/shard_map/jit(_take)/gather | solution.py:84
  446.4 3.5 fusion.8
  (83 shorter events, 18.0 us)
Async XLA Ops:
  6.5 8.4 %copy-start = (bf16[128,2048]{1,0:T(8,128)(2,1)S(1)}, bf16[128,2048]{1,0:T(8,128)(2,1)}, u32[]{:S(2)}) copy-start(bf16[128,2048]{1,0:T(8,128)(2,1)} %param.8) | copy-start | bytes 1572868
  6.5 8.5 %copy-start.5 = (f32[2048]{0:T(1024)S(1)}, f32[2048]{0:T(1024)}, u32[]{:S(2)}) copy-start(f32[2048]{0:T(1024)} %param.9) | copy-start | bytes 24580
  6.5 132.2 %all-gather.2.cloned.1.call-start = ((), (), s32[]{:S(2)}) async-start(), calls=%async_computation.8 | async-start | bytes 18382848 | tf_op jit(solution)/shard_map/all_gather | solution.py:51
  16.1 208.2 %reduce-scatter.5.cloned.1.call-start = ((), (), s32[]{:S(2)}) async-start(), calls=%async_computation.9 | async-start | bytes 6553600 | tf_op jit(solution)/shard_map/reduce_scatter | solution.py:77
  174.0 103.9 %reduce-scatter.7.cloned.1.call-start = ((), (), s32[]{:S(2)}) async-start(), calls=%async_computation.10 | async-start | bytes 6553600 | tf_op jit(solution)/shard_map/reduce_scatter | solution.py:77
  224.2 1.3 copy-start.2
  229.1 39.7 %all-to-all-start = ((bf16[8,40,2048]{2,1,0:T(8,128)(2,1)}), bf16[8,40,2048]{2,1,0:T(8,128)(2,1)S(1)}, u32[]{:S(2)}, u32[]{:S(2)}) async-start(bf16[8,40,2048]{2,1,0:T(8,128)(2,1)} %copy.79), calls=%async_computation.1 | async-start | bytes 2621440 | tf_op jit(solution)/shard_map/all_to_all | solution.py:81
  234.1 97.6 %reduce-scatter.9.cloned.1.call-start = ((), (), s32[]{:S(2)}) async-start(), calls=%async_computation.11 | async-start | bytes 6553600 | tf_op jit(solution)/shard_map/reduce_scatter | solution.py:77
  277.8 1.3 copy-start.1
  282.7 40.1 %all-to-all-start.1 = ((bf16[8,40,2048]{2,1,0:T(8,128)(2,1)}), bf16[8,40,2048]{2,1,0:T(8,128)(2,1)S(1)}, u32[]{:S(2)}, u32[]{:S(2)}) async-start(bf16[8,40,2048]{2,1,0:T(8,128)(2,1)} %copy.85), calls=%async_computation.3 | async-start | bytes 2621440 | tf_op jit(solution)/shard_map/all_to_all | solution.py:81
  288.2 97.4 %reduce-scatter.11.cloned.1.call-start = ((), (), s32[]{:S(2)}) async-start(), calls=%async_computation.12 | async-start | bytes 6553600 | tf_op jit(solution)/shard_map/reduce_scatter | solution.py:77
  336.6 53.9 %all-to-all-start.2 = ((bf16[8,40,2048]{2,1,0:T(8,128)(2,1)}), bf16[8,40,2048]{2,1,0:T(8,128)(2,1)}, u32[]{:S(2)}, u32[]{:S(2)}) async-start(bf16[8,40,2048]{2,1,0:T(8,128)(2,1)} %copy.91), calls=%async_computation.5 | async-start | bytes 2621440 | tf_op jit(solution)/shard_map/all_to_all | solution.py:81
  388.0 8.2 %copy-start.4 = (f32[128,8]{0,1:T(8,128)S(1)}, f32[128,8]{0,1:T(8,128)}, u32[]{:S(2)}) copy-start(f32[128,8]{0,1:T(8,128)} %param.11) | copy-start | bytes 12292
  388.0 8.4 %copy-start.3 = (s32[128,8]{0,1:T(8,128)S(1)}, s32[128,8]{0,1:T(8,128)}, u32[]{:S(2)}) copy-start(s32[128,8]{0,1:T(8,128)} %param.10) | copy-start | bytes 12292
  390.5 37.9 %all-to-all-start.3 = ((bf16[8,40,2048]{2,1,0:T(8,128)(2,1)}), bf16[8,40,2048]{2,1,0:T(8,128)(2,1)}, u32[]{:S(2)}, u32[]{:S(2)}) async-start(bf16[8,40,2048]{2,1,0:T(8,128)(2,1)} %copy.97), calls=%async_computation.7 | async-start | bytes 2621440 | tf_op jit(solution)/shard_map/all_to_all | solution.py:81
Sparse Core Ops, SparseCore 0:
  16.2 122.5 all-gather.1
  174.1 49.5 reduce-scatter.4
  226.4 51.4 reduce-scatter.6
  280.2 51.3 reduce-scatter.8
  334.2 51.3 reduce-scatter.10
where the time goes:
time: 467 us; the launch traced here: 458 us
  waiting for transfers between devices  216 us (46%)
  local copies, waits for them, and re-layouts  138 us (30%)
  matrix products  58.2 us (12%)
  starting transfers between devices  22.7 us (5%)
  between operations  13.7 us (3%)
  other arithmetic  9.89 us (2%)
    all_gather x1, waiting for transfers between devices, local(): every = lax.all_gather(packed, ALL, axis=0, tiled=True)  123 us
    gather x4, local copies, waits for them, and re-layouts, local(): picked = jnp.take(every, rows[span].reshape(-1), axis=0, mode='clip')  79.9 us
    reduce_scatter x4, waiting for transfers between devices, local(): lax.psum_scatter(partial, 'tok', scatter_dimension=1, tiled=True)  61.2 us
    all_to_all x4, waiting for transfers between devices, local(): lax.all_to_all(summed, ('row', 'col'), split_axis=0, concat_axis=0, tiled...  31.9 us
    dot_general x4, matrix products, local(): jnp.einsum('jrd,jgfd->jrgf', picked, gate_up_weight[span], preferred_elem...  31.4 us
    dot_general x4, matrix products, local(): jnp.einsum('jrf,jfd->jrd', hidden, down_weight[span], preferred_element_t...  23.3 us
    all_to_all x4, starting transfers between devices, local(): lax.all_to_all(summed, ('row', 'col'), split_axis=0, concat_axis=0, tiled...  21.7 us
    slice x1, local copies, waits for them, and re-layouts, local(): gate_up_weight[span]  16.3 us
  transfers between devices with their start and end apart: 9, of which 5 were waited for; matrix products, arithmetic and copies ran while one was open for 30% of the time, Pallas kernels for 0%

commit v1 on v0

--- a/solution.py
+++ b/solution.py
@@ -8,6 +8,24 @@
 PIECES = 4
 EPSILON = 1e-06
 ALL = ("row", "col", "tok")
+
+
+def in_order(tiles, dim):
+    shape = list(tiles.shape[1:])
+    shape[dim] *= tiles.shape[0]
+    return jnp.moveaxis(tiles, 0, dim).reshape(shape)
+
+
+def doubled(array, axis):
+    length = lax.axis_size(axis)
+    pieces = array[None]
+    for level in range(length.bit_length() - 1):
+        bit = 1 << level
+        theirs = lax.ppermute(pieces, axis, [(i, i ^ bit) for i in range(length)])
+        both = jnp.stack([pieces, theirs])
+        upper = lax.axis_index(axis) >> level & 1
+        pieces = jnp.where(upper == 0, both, both[::-1]).reshape(-1, *array.shape)
+    return pieces
 
 
 def rank_in_block(block_routes, experts):
@@ -48,7 +66,7 @@
     table_rows = jnp.zeros((extra * features,), jnp.bfloat16)
     table_rows = table_rows.at[: experts * CAP].set(source.astype(jnp.bfloat16))
     packed = jnp.concatenate([normed, table_rows.reshape(extra, features)], axis=0)
-    every = lax.all_gather(packed, ALL, axis=0, tiled=True)
+    every = in_order(doubled(packed, ALL), 0)
     tables = every.reshape(devices, stride, features)[:, count:, :].reshape(devices, -1)
     tables = lax.dynamic_slice_in_dim(
         tables[:, : experts * CAP], owner * holding * CAP, holding * CAP, axis=1

time: 467 us -> 866 us (1.85)
  waiting for transfers between devices: 216 us -> 554 us
  other arithmetic: 9.89 us -> 55.7 us
  starting transfers between devices: 22.7 us -> 31.7 us
    ppermute x0 -> x5, waiting for transfers between devices: none -> 458 us  [doubled(): theirs = lax.ppermute(pieces, axis, [(i, i ^ bit) for i in range(length)])]
    all_gather x1 -> x0, waiting for transfers between devices: 123 us -> none  [local(): every = lax.all_gather(packed, ALL, axis=0, tiled=True)]
    select_n x0 -> x4, other arithmetic: none -> 26.8 us  [doubled(): pieces = jnp.where(upper == 0, both, both[::-1]).reshape(-1, *array.shape)]
    another operation x3 -> x10, other arithmetic: 0.27 us -> 19.5 us  [the longest x7 19.3 us: doubled(): both = jnp.stack([pieces, theirs])]
    ppermute x0 -> x5, starting transfers between devices: none -> 8.88 us  [doubled(): theirs = lax.ppermute(pieces, axis, [(i, i ^ bit) for i in range(length)])]
  transfers between devices with their start and end apart: 9 -> 13, of which waited for: 5 -> 10; matrix products, arithmetic and copies ran while one was open for 30% -> 16% of each run, Pallas kernels for 0% -> 0%
where the time goes in v1:
time: 866 us; the launch traced here: 857 us
  waiting for transfers between devices  554 us (64%)
  local copies, waits for them, and re-layouts  143 us (17%)
  matrix products  58.3 us (7%)
  other arithmetic  55.7 us (6%)
  starting transfers between devices  31.7 us (4%)
  between operations  14 us (2%)
    ppermute x5, waiting for transfers between devices, doubled(): theirs = lax.ppermute(pieces, axis, [(i, i ^ bit) for i in range(length)])  458 us
    gather x4, local copies, waits for them, and re-layouts, local(): picked = jnp.take(every, rows[span].reshape(-1), axis=0, mode='clip')  80.1 us
    reduce_scatter x4, waiting for transfers between devices, local(): lax.psum_scatter(partial, 'tok', scatter_dimension=1, tiled=True)  64.1 us
    all_to_all x4, waiting for transfers between devices, local(): lax.all_to_all(summed, ('row', 'col'), split_axis=0, concat_axis=0, tiled...  31.8 us
    dot_general x4, matrix products, local(): jnp.einsum('jrd,jgfd->jrgf', picked, gate_up_weight[span], preferred_elem...  31.5 us
    select_n x4, other arithmetic, doubled(): pieces = jnp.where(upper == 0, both, both[::-1]).reshape(-1, *array.shape)  26.8 us
    dot_general x4, matrix products, local(): jnp.einsum('jrf,jfd->jrd', hidden, down_weight[span], preferred_element_t...  23.3 us
    all_to_all x4, starting transfers between devices, local(): lax.all_to_all(summed, ('row', 'col'), split_axis=0, concat_axis=0, tiled...  22.3 us
  transfers between devices with their start and end apart: 13, of which 10 were waited for; matrix products, arithmetic and copies ran while one was open for 16% of the time, Pallas kernels for 0%

profile of v1, /device:TPU:0, one launch (start us, length us, event | category | flops | bytes accessed | tf_op | source)
XLA Modules:
  0.0 856.8 jit_solution(4059496062673325609)
XLA Ops:
  22.2 24.9 %collective-permute-done.1 = bf16[2,136,2048]{2,1,0:T(8,128)(2,1)S(1)} collective-permute-done((bf16[2,136,2048]{2,1,0:T(8,128)(2,1)S(1)}, bf16[2,136,2048]{2,1,0:T(8,128)(2,1)S(1)}, u32[]{:S(2)}, u32[]{:S(2)}) %collective-permute-start.1) | collective-permute-done | bytes 1114144 | tf_op jit(solution)/shard_map/ppermute | solution.py:24
  49.7 48.3 %collective-permute-done.2 = bf16[4,136,2048]{2,1,0:T(8,128)(2,1)} collective-permute-done((bf16[4,136,2048]{2,1,0:T(8,128)(2,1)S(1)}, bf16[4,136,2048]{2,1,0:T(8,128)(2,1)}, u32[]{:S(2)}, u32[]{:S(2)}) %collective-permute-start.2) | collective-permute-done | bytes 2228256 | tf_op jit(solution)/shard_map/ppermute | solution.py:24
  105.9 191.0 %collective-permute-done.3 = bf16[8,136,2048]{2,1,0:T(8,128)(2,1)} collective-permute-done((bf16[8,136,2048]{2,1,0:T(8,128)(2,1)}, bf16[8,136,2048]{2,1,0:T(8,128)(2,1)}, u32[]{:S(2)}, u32[]{:S(2)}) %collective-permute-start.3) | collective-permute-done | bytes 4456480 | tf_op jit(solution)/shard_map/ppermute | solution.py:24
  296.9 7.9 pad_maximum_fusion.1
  304.8 15.0 %reverse_select_fusion.1 = bf16[2,8,136,2048]{3,2,1,0:T(8,128)(2,1)} fusion(bf16[2,8,136,2048]{3,2,1,0:T(8,128)(2,1)} %pad_maximum_fusion.1, pred[]{:T(512)S(6)} %eq.46), kind=kLoop, calls=%fused_computation.8 | loop fusion | flops 4456448 | bytes 17825792 | tf_op jit(solution)/shard_map/jit(_where)/select_n | solution.py:27
  320.9 192.2 %collective-permute-done.4 = bf16[16,136,2048]{2,1,0:T(8,128)(2,1)} collective-permute-done((bf16[16,136,2048]{2,1,0:T(8,128)(2,1)}, bf16[16,136,2048]{2,1,0:T(8,128)(2,1)}, u32[]{:S(2)}, u32[]{:S(2)}) %collective-permute-start.4) | collective-permute-done | bytes 8912928 | tf_op jit(solution)/shard_map/ppermute | solution.py:24
  513.1 8.5 pad_maximum_fusion
  521.6 7.9 reverse_select_fusion
  529.5 6.1 copy-done
  536.8 19.2 %gather_fusion = bf16[1280,2048]{1,0:T(8,128)(2,1)} fusion(bf16[4352,2048]{1,0:T(8,128)(2,1)} %bitcast.140, s32[2048]{0:T(1024)S(1)} %pad_clamp_fusion.3), kind=kCustom, calls=%fused_computation | custom fusion | bytes 10490880 | tf_op jit(solution)/shard_map/jit(_take)/gather | solution.py:83
  556.0 7.8 fusion.6
  563.8 5.7 convolution_convert_fusion.3
  569.6 16.0 %fusion.53 = (bf16[4,2,192,2048]{3,2,1,0:T(8,128)(2,1)}, bf16[4,2,192,2048]{3,2,1,0:T(8,128)(2,1)}, bf16[4,2,192,2048]{3,2,1,0:T(8,128)(2,1)}) fusion(bf16[16,2,192,2048]{3,2,1,0:T(8,128)(2,1)} %param.12), kind=kLoop, calls=%fused_computation.105 | loop fusion | bytes 37748736 | tf_op jit(solution)/shard_map/slice | solution.py:86
  585.8 20.1 %gather_fusion.1 = bf16[1280,2048]{1,0:T(8,128)(2,1)} fusion(bf16[4352,2048]{1,0:T(8,128)(2,1)} %bitcast.141, s32[2048]{0:T(1024)S(1)} %pad_clamp_fusion.2), kind=kCustom, calls=%fused_computation.1 | custom fusion | bytes 10490880 | tf_op jit(solution)/shard_map/jit(_take)/gather | solution.py:83
  605.9 7.9 fusion.4
  613.8 5.8 convolution_convert_fusion.2
  627.3 5.5 all-to-all-start
  633.2 20.5 %gather_fusion.2 = bf16[1280,2048]{1,0:T(8,128)(2,1)} fusion(bf16[4352,2048]{1,0:T(8,128)(2,1)} %bitcast.142, s32[2048]{0:T(1024)S(1)} %pad_clamp_fusion.1), kind=kCustom, calls=%fused_computation.2 | custom fusion | bytes 10490880 | tf_op jit(solution)/shard_map/jit(_take)/gather | solution.py:83
  653.7 7.9 fusion.2
  661.6 5.9 convolution_convert_fusion.1
  667.5 9.1 %reduce-scatter.7.cloned.1.call-done = bf16[4,80,2048]{2,1,0:T(8,128)(2,1)} async-done(((bf16[4,320,2048]{2,1,0:T(8,128)(2,1)}), bf16[4,80,2048]{2,1,0:T(8,128)(2,1)}) %reduce-scatter.7.cloned.1.call-update) | async-done | bytes 1310736 | tf_op jit(solution)/shard_map/reduce_scatter | solution.py:95
  681.4 5.5 all-to-all-start.1
  687.3 20.3 %gather_fusion.3 = bf16[1280,2048]{1,0:T(8,128)(2,1)} fusion(bf16[4352,2048]{1,0:T(8,128)(2,1)} %bitcast.143, s32[2048]{0:T(1024)S(1)} %pad_clamp_fusion), kind=kCustom, calls=%fused_computation.3 | custom fusion | bytes 10490880 | tf_op jit(solution)/shard_map/jit(_take)/gather | solution.py:83
  707.7 7.9 fusion
  715.6 5.9 convolution_convert_fusion
  721.5 9.0 %reduce-scatter.9.cloned.1.call-done = bf16[4,80,2048]{2,1,0:T(8,128)(2,1)} async-done(((bf16[4,320,2048]{2,1,0:T(8,128)(2,1)}), bf16[4,80,2048]{2,1,0:T(8,128)(2,1)}) %reduce-scatter.9.cloned.1.call-update) | async-done | bytes 1310736 | tf_op jit(solution)/shard_map/reduce_scatter | solution.py:95
  735.4 5.8 all-to-all-start.2
  741.2 43.2 %reduce-scatter.11.cloned.1.call-done = bf16[4,80,2048]{2,1,0:T(8,128)(2,1)} async-done(((bf16[4,320,2048]{2,1,0:T(8,128)(2,1)}), bf16[4,80,2048]{2,1,0:T(8,128)(2,1)}) %reduce-scatter.11.cloned.1.call-update) | async-done | bytes 1310736 | tf_op jit(solution)/shard_map/reduce_scatter | solution.py:95
  789.4 5.5 all-to-all-start.3
  795.4 31.8 %all-to-all-done.3 = bf16[8,40,2048]{2,1,0:T(8,128)(2,1)} async-done(((bf16[8,40,2048]{2,1,0:T(8,128)(2,1)}), bf16[8,40,2048]{2,1,0:T(8,128)(2,1)}, u32[]{:S(2)}, u32[]{:S(2)}) %all-to-all-start.3) | async-done | bytes 1310752 | tf_op jit(solution)/shard_map/all_to_all | solution.py:99
  827.2 6.0 pad_maximum_fusion.2
  833.2 12.0 %gather_fusion.4 = bf16[1024,2048]{1,0:T(8,128)(2,1)} fusion(bf16[1280,2048]{1,0:T(8,128)(2,1)} %bitcast.144, s32[1024]{0:T(1024)S(1)} %broadcast_clamp_fusion), kind=kCustom, calls=%fused_computation.4 | custom fusion | bytes 8392704 | tf_op jit(solution)/shard_map/jit(_take)/gather | solution.py:102
  (108 shorter events, 56.6 us)
Async XLA Ops:
  6.5 9.0 %copy-start.1 = (bf16[128,2048]{1,0:T(8,128)(2,1)S(1)}, bf16[128,2048]{1,0:T(8,128)(2,1)}, u32[]{:S(2)}) copy-start(bf16[128,2048]{1,0:T(8,128)(2,1)} %param.8) | copy-start | bytes 1572868
  6.5 615.9 %reduce-scatter.5.cloned.1.call-start = ((), (), s32[]{:S(2)}) async-start(), calls=%async_computation.8 | async-start | bytes 6553600 | tf_op jit(solution)/shard_map/reduce_scatter | solution.py:95
  10.6 0.6 copy-start.4
  11.2 4.3 copy-start.7
  16.6 2.1 collective-permute-start
  19.3 27.8 %collective-permute-start.1 = (bf16[2,136,2048]{2,1,0:T(8,128)(2,1)S(1)}, bf16[2,136,2048]{2,1,0:T(8,128)(2,1)S(1)}, u32[]{:S(2)}, u32[]{:S(2)}) collective-permute-start(bf16[2,136,2048]{2,1,0:T(8,128)(2,1)S(1)} %get-tuple-element.27), channel_id=1, source_target_pairs={{0,2},{1,3},{2,0},{3,1},{4,6},{5,7},{6,4},{7,5},{8,10},{9,11},{10,... | collective-permute-start | bytes 3342344 | tf_op jit(solution)/shard_map/ppermute | solution.py:24
  47.8 50.1 %collective-permute-start.2 = (bf16[4,136,2048]{2,1,0:T(8,128)(2,1)S(1)}, bf16[4,136,2048]{2,1,0:T(8,128)(2,1)}, u32[]{:S(2)}, u32[]{:S(2)}) collective-permute-start(bf16[4,136,2048]{2,1,0:T(8,128)(2,1)S(1)} %bitcast.147), channel_id=1, source_target_pairs={{0,4},{1,5},{2,6},{3,7},{4,0},{5,1},{6,2},{7,3},{8,12},{9,13},{10,... | collective-permute-start | bytes 6684680 | tf_op jit(solution)/shard_map/ppermute | solution.py:24
  103.4 193.5 %collective-permute-start.3 = (bf16[8,136,2048]{2,1,0:T(8,128)(2,1)}, bf16[8,136,2048]{2,1,0:T(8,128)(2,1)}, u32[]{:S(2)}, u32[]{:S(2)}) collective-permute-start(bf16[8,136,2048]{2,1,0:T(8,128)(2,1)} %bitcast.16), channel_id=1, source_target_pairs={{0,8},{1,9},{2,10},{3,11},{4,12},{5,13},{6,14},{7,15},{8,0},{9,1},... | collective-permute-start | bytes 13369352 | tf_op jit(solution)/shard_map/ppermute | solution.py:24
  319.8 193.3 %collective-permute-start.4 = (bf16[16,136,2048]{2,1,0:T(8,128)(2,1)}, bf16[16,136,2048]{2,1,0:T(8,128)(2,1)}, u32[]{:S(2)}, u32[]{:S(2)}) collective-permute-start(bf16[16,136,2048]{2,1,0:T(8,128)(2,1)} %bitcast.145), channel_id=1, source_target_pairs={{0,16},{1,17},{2,18},{3,19},{4,20},{5,21},{6,22},{7,23},{8,24},{9,... | collective-permute-start | bytes 26738696 | tf_op jit(solution)/shard_map/ppermute | solution.py:24
  529.5 6.1 copy-start
  569.6 107.0 %reduce-scatter.7.cloned.1.call-start = ((), (), s32[]{:S(2)}) async-start(), calls=%async_computation.9 | async-start | bytes 6553600 | tf_op jit(solution)/shard_map/reduce_scatter | solution.py:95
  622.4 1.3 copy-start.3
  627.3 40.2 %all-to-all-start = ((bf16[8,40,2048]{2,1,0:T(8,128)(2,1)}), bf16[8,40,2048]{2,1,0:T(8,128)(2,1)S(1)}, u32[]{:S(2)}, u32[]{:S(2)}) async-start(bf16[8,40,2048]{2,1,0:T(8,128)(2,1)} %copy.79), calls=%async_computation.1 | async-start | bytes 2621440 | tf_op jit(solution)/shard_map/all_to_all | solution.py:99
  632.8 97.7 %reduce-scatter.9.cloned.1.call-start = ((), (), s32[]{:S(2)}) async-start(), calls=%async_computation.10 | async-start | bytes 6553600 | tf_op jit(solution)/shard_map/reduce_scatter | solution.py:95
  676.5 1.3 copy-start.2
  681.4 40.1 %all-to-all-start.1 = ((bf16[8,40,2048]{2,1,0:T(8,128)(2,1)}), bf16[8,40,2048]{2,1,0:T(8,128)(2,1)S(1)}, u32[]{:S(2)}, u32[]{:S(2)}) async-start(bf16[8,40,2048]{2,1,0:T(8,128)(2,1)} %copy.85), calls=%async_computation.3 | async-start | bytes 2621440 | tf_op jit(solution)/shard_map/all_to_all | solution.py:99
  686.9 97.6 %reduce-scatter.11.cloned.1.call-start = ((), (), s32[]{:S(2)}) async-start(), calls=%async_computation.11 | async-start | bytes 6553600 | tf_op jit(solution)/shard_map/reduce_scatter | solution.py:95
  735.4 54.0 %all-to-all-start.2 = ((bf16[8,40,2048]{2,1,0:T(8,128)(2,1)}), bf16[8,40,2048]{2,1,0:T(8,128)(2,1)}, u32[]{:S(2)}, u32[]{:S(2)}) async-start(bf16[8,40,2048]{2,1,0:T(8,128)(2,1)} %copy.91), calls=%async_computation.5 | async-start | bytes 2621440 | tf_op jit(solution)/shard_map/all_to_all | solution.py:99
  786.8 8.1 copy-start.5
  786.8 8.2 copy-start.9
  786.8 8.4 copy-start.6
  786.8 8.6 %copy-start.8 = (s32[1024,1]{0,1:T(1,128)S(1)}, s32[1024,1]{0,1:T(1,128)}, u32[]{:S(2)}) copy-start(s32[1024,1]{0,1:T(1,128)} %copy-done.7) | copy-start | bytes 12292
  789.4 37.9 %all-to-all-start.3 = ((bf16[8,40,2048]{2,1,0:T(8,128)(2,1)}), bf16[8,40,2048]{2,1,0:T(8,128)(2,1)}, u32[]{:S(2)}, u32[]{:S(2)}) async-start(bf16[8,40,2048]{2,1,0:T(8,128)(2,1)} %copy.97), calls=%async_computation.7 | async-start | bytes 2621440 | tf_op jit(solution)/shard_map/all_to_all | solution.py:99
Sparse Core Ops, SparseCore 0:
  569.7 52.7 reduce-scatter.4
  625.1 51.3 reduce-scatter.6
  679.1 51.3 reduce-scatter.8
  733.0 51.3 reduce-scatter.10
